TPU v7x, 32 devices: a whole 2x2x4 slice. The times are simulated.
32 devices in a mesh: row: 4 (over y, x), col: 8 (over z, core).
Axes of the slice: x: 2, y: 2, z: 4, core: 2. Of those that a mesh axis runs over, the one named last changes fastest.
Arguments:
- covariance: float32 [20, 4, 10, 8, 256, 256], P(None, 'row', None, 'col'), may hold values from -0.006 to 2.4, as said below
- telemetry: bfloat16 [1536, 10, 8, 256], P('row', None, 'col'), may hold values from -6 to 6
- active: int32 [8, 1280], replicated, may hold values 0 or 1
- panel: int32 [1], replicated, may hold values from 0 to 75
Outputs:
- factored: float32 [20, 4, 10, 8, 256, 256], P(None, 'row', None, 'col')
Inputs may be any that keep to these rules, and one draw needn't show every extreme that they name: `covariance`: in every diagonal tile each diagonal entry exceeds the sum of magnitudes of the other entries of its row; entries off the matrix diagonal lie in -0.006 to 0.006.
All inputs are finite; a program needn't handle non-finite values.
Results may differ from a plain program's by a relative error of at most 0.0006.
Values may be sent and summed in bfloat16 or wider, within the bound.
No kernel may reach another device: no remote copies, remote signals or barrier semaphores. Data moves between devices by JAX's collectives and lax.ppermute only.
A program may use at most 384 MiB of HBM per device.

v0:
```python
import jax
import jax.numpy as jnp
from jax import lax
from jax.sharding import PartitionSpec as P

FORGET = 0.9


def from_root(block, axis, holder):
    block = jnp.where(lax.axis_index(axis) == holder, block, jnp.zeros_like(block))
    return lax.psum(block, axis)


def body(covariance, telemetry, active, panel):
    n_row = lax.axis_size("row")
    n_col = lax.axis_size("col")
    row_index = lax.axis_index("row")
    col_index = lax.axis_index("col")
    blocks_a = covariance.shape[0]
    blocks_b = covariance.shape[2]
    width = covariance.shape[4]
    ratio = n_col // n_row
    samples = telemetry.shape[0] * n_row
    tiles = blocks_b * n_col
    earlier = covariance[:, 0, :, 0]
    local = telemetry[:, :, 0, :]
    mask_full = jnp.concatenate([active, active], axis=1).reshape(tiles, width).astype(jnp.bfloat16)
    col_mask = lax.dynamic_index_in_dim(
        mask_full.reshape(blocks_b, n_col, width), col_index, 1, keepdims=False
    )
    row_mask = lax.dynamic_index_in_dim(
        mask_full.reshape(blocks_a, n_row, width), row_index, 1, keepdims=False
    )
    column_data = lax.all_gather(local, "row", axis=0, tiled=True)
    slabs = []
    for offset in range(ratio):
        slabs.append(from_root(column_data, "col", row_index + offset * n_row))
    row_data = jnp.stack(slabs, axis=2).reshape(samples, blocks_a, width)
    column_data = column_data * col_mask[None]
    row_data = row_data * row_mask[None]
    row_tiles = jnp.arange(blocks_a, dtype=jnp.int32) * n_row + row_index
    col_tiles = jnp.arange(blocks_b, dtype=jnp.int32) * n_col + col_index
    lower = row_tiles[:, None] >= col_tiles[None, :]
    gram = jnp.einsum("sat,sbu->abtu", row_data, column_data, preferred_element_type=jnp.float32)
    fresh = jnp.where(lower[:, :, None, None], FORGET * earlier + gram / samples, earlier)
    panel_at = panel[0]
    owner_row = panel_at % n_row
    owner_col = panel_at % n_col
    diag_tile = lax.dynamic_slice(
        fresh, (panel_at // n_row, panel_at // n_col, 0, 0), (1, 1, width, width)
    )[0, 0]
    factor = jnp.linalg.cholesky(diag_tile)
    inverse = lax.linalg.triangular_solve(
        factor, jnp.eye(width, dtype=jnp.float32), left_side=True, lower=True
    )
    inverse = from_root(inverse, "row", owner_row)
    column_part = lax.dynamic_index_in_dim(fresh, panel_at // n_col, 1, keepdims=False)
    solved = jnp.einsum(
        "atu,vu->atv",
        column_part,
        inverse,
        precision=lax.Precision.HIGHEST,
        preferred_element_type=jnp.float32,
    )
    solved = jnp.where((row_tiles > panel_at)[:, None, None], solved, jnp.zeros_like(solved))
    panel_rows = from_root(solved.astype(jnp.bfloat16), "col", owner_col).astype(solved.dtype)
    pick = col_index // n_row
    chosen = lax.dynamic_index_in_dim(
        panel_rows.reshape(blocks_b, ratio, width, width), pick, 1, keepdims=False
    )
    panel_cols = from_root(chosen.astype(jnp.bfloat16), "row", col_index % n_row).astype(
        chosen.dtype
    )
    trailing = lower & (col_tiles[None, :] > panel_at)
    update = jnp.einsum(
        "atv,buv->abtu",
        panel_rows,
        panel_cols,
        precision=lax.Precision.HIGHEST,
        preferred_element_type=jnp.float32,
    )
    result = jnp.where(trailing[:, :, None, None], fresh - update, fresh)
    on_column = (col_tiles == panel_at)[None, :] & (row_tiles > panel_at)[:, None]
    result = jnp.where(on_column[:, :, None, None], panel_rows[:, None], result)
    on_diagonal = (col_tiles == panel_at)[None, :] & (row_tiles == panel_at)[:, None]
    result = jnp.where(on_diagonal[:, :, None, None], factor[None, None], result)
    return result[:, None, :, None]


def solution(mesh):
    in_specs = (P(None, "row", None, "col", None, None), P("row", None, "col", None), P(), P())
    out_specs = P(None, "row", None, "col", None, None)
    return jax.shard_map(body, mesh=mesh, in_specs=in_specs, out_specs=out_specs, check_vma=False)
```

profile of v0, /device:TPU:0, one launch (start us, length us, event | category | flops | bytes accessed | tf_op | source)
XLA Modules:
  0.0 831.1 jit_solution(5645800348601662963)
XLA Ops:
  6.5 0.7 all-gather.3.cloned.1.call-update
  7.3 87.7 %all-gather.3.cloned.1.call-done = bf16[1536,10,1,256]{3,0,1,2:T(8,128)(2,1)} async-done(((bf16[384,10,1,256]{3,0,1,2:T(8,128)(2,1)}), bf16[1536,10,1,256]{3,0,1,2:T(8,128)(2,1)}) %all-gather.3.cloned.1.call-update) | async-done | bytes 7864336 | tf_op jit(solution)/shard_map/all_gather | solution.py:34
  95.0 9.7 %fusion.6 = (bf16[1536,10,1,256]{3,0,1,2:T(8,128)(2,1)}, bf16[1536,10,1,256]{3,0,2,1:T(8,128)(2,1)}) fusion(bf16[1536,10,1,256]{3,0,1,2:T(8,128)(2,1)} %all-gather.3.cloned.1.call-done, pred[]{:T(512)S(6)} %eq.50, pred[]{:T(512)S(6)} %eq.51), kind=kLoop, calls=%fused_computation.16 | loop fusion | flops 7864320 | bytes 23592962 | tf_op jit(solution)/shard_map/stack | solution.py:38
  105.8 49.6 %copy.22 = f32[20,1,10,1,256,256]{4,5,0,2,3,1:T(8,128)} copy(f32[20,1,10,1,256,256]{5,4,3,2,1,0:T(8,128)} %param.4) | data formatting | bytes 104857600 | tf_op args[0]
  155.6 263.2 %all-reduce.13.cloned.1.call-done = (bf16[1536,10,1,256]{3,0,2,1:T(8,128)(2,1)}, bf16[1536,10,1,256]{3,0,1,2:T(8,128)(2,1)}) async-done(((bf16[1536,10,1,256]{3,0,2,1:T(8,128)(2,1)}, bf16[1536,10,1,256]{3,0,1,2:T(8,128)(2,1)}), (bf16[1536,10,1,256]{3,0,2,1:T(8,128)(2,1)}, bf16[1536,10,1,256]{3,0,1,2:T(8,128)(2,1)})) %all-reduce.13.cloned.1.call-update) | async-done | bytes 15728656 | tf_op jit(solution)/shard_map/psum | solution.py:11
  418.8 7.8 pad_maximum_fusion
  426.6 6.5 bitcast_multiply_fusion.1
  433.1 56.1 %fusion.3 = f32[20,10,256,256]{2,3,0,1:T(8,128)} fusion(f32[20,1,10,1,256,256]{4,5,0,2,3,1:T(8,128)} %copy.22, pred[20,10]{0,1:T(8,128)(4,1)S(1)} %get-tuple-element.34, bf16[1536,20,256]{2,0,1:T(8,128)(2,1)} %bitcast_multiply_fusion.1, bf16[1536,10,1,256]{3,0,1,2:T(8,128)(2,1)} %all-gather.3.cloned.1.call-done, bf16[10,256]{1,0:T(8,128)(2,1)S(1)} %bitcast.126), kind=kOutput, calls=%fused_computation.7 | convolution fusion | flops 40333475840 | bytes 128455880 | tf_op jit(solution)/shard_map/sat,sbu->abtu/dot_general | solution.py:44
  489.2 1.0 dynamic-slice_bitcast_fusion
  490.3 1.0 fusion.19
  491.3 11.7 %cholesky.50 = f32[128,128]{1,0:T(8,128)S(1)} custom-call(f32[128,128]{1,0:T(8,128)S(1)} %cholesky.118), custom_call_target="Cholesky" | custom-call | tf_op jit(solution)/shard_map/jit(cholesky)/cholesky | solution.py:52
  503.1 9.8 %custom-call.14 = f32[1,128,128]{1,2,0:T(8,128)S(1)} custom-call(f32[1,128,128]{2,1,0:T(8,128)S(1)} %get-tuple-element.32), custom_call_target="InvertDiagBlocksLowerTriangular" | custom-call | tf_op jit(solution)/shard_map/jit(cholesky)/cholesky | solution.py:52
  513.1 0.3 convolution_subtract_fusion.1
  513.4 11.7 %cholesky.105 = f32[128,128]{1,0:T(8,128)S(1)} custom-call(f32[128,128]{1,0:T(8,128)S(1)} %convolution_subtract_fusion.1), custom_call_target="Cholesky" | custom-call | tf_op jit(solution)/shard_map/jit(cholesky)/cholesky | solution.py:52
  525.2 0.7 compare_reduce_fusion
  527.3 3.9 while.1
  527.3 0.6 fusion.39
  527.9 1.3 bitcast_dynamic-update-slice_fusion.2
  529.2 0.6 fusion.39
  529.8 1.3 bitcast_dynamic-update-slice_fusion.2
  531.2 19.9 %custom-call.15 = f32[2,128,128]{1,2,0:T(8,128)S(1)} custom-call(f32[2,128,128]{2,1,0:T(8,128)S(1)} %get-tuple-element.12), custom_call_target="InvertDiagBlocksLowerTriangular" | custom-call | tf_op jit(solution)/shard_map/triangular_solve | solution.py:53
  551.1 0.3 fusion.22
  551.6 0.3 fusion.25
  551.9 0.7 maximum_select_fusion
  552.8 43.4 %all-reduce.7.cloned.1.call-done = f32[256,256]{1,0:T(8,128)} async-done(((f32[256,256]{1,0:T(8,128)}), f32[256,256]{1,0:T(8,128)}) %all-reduce.7.cloned.1.call-update) | async-done | bytes 262160 | tf_op jit(solution)/shard_map/psum | solution.py:11
  596.1 12.9 %fusion.12 = bf16[20,256,256]{2,1,0:T(8,128)(2,1)} fusion(pred[20]{0:T(512)(128)(4,1)S(1)} %broadcast_compare_fusion.1, pred[]{:T(512)S(6)} %eq.52, f32[20,10,256,256]{2,3,0,1:T(8,128)} %fusion.3, s32[]{:T(128)S(6)} %select_n.120, f32[256,256]{1,0:T(8,128)} %all-reduce.7.cloned.1.call-done), kind=kOutput, calls=%fused_computation.23 | convolution fusion | flops 4030464000 | bytes 8126489 | tf_op jit(solution)/shard_map/atu,vu->atv/dot_general | solution.py:58
  609.1 69.2 %all-reduce.9.cloned.1.call-done = bf16[20,256,256]{2,1,0:T(8,128)(2,1)} async-done(((bf16[20,256,256]{2,1,0:T(8,128)(2,1)}), bf16[20,256,256]{2,1,0:T(8,128)(2,1)}) %all-reduce.9.cloned.1.call-update) | async-done | bytes 2621456 | tf_op jit(solution)/shard_map/psum | solution.py:11
  678.3 2.6 fusion.17
  681.2 5.1 copy.29
  686.4 50.4 %all-reduce.11.cloned.1.call-done = bf16[10,256,256]{2,1,0:T(8,128)(2,1)} async-done(((bf16[10,256,256]{2,1,0:T(8,128)(2,1)}), bf16[10,256,256]{2,1,0:T(8,128)(2,1)}) %all-reduce.11.cloned.1.call-update) | async-done | bytes 1310736 | tf_op jit(solution)/shard_map/psum | solution.py:11
  736.8 35.7 %fusion.2 = f32[20,1,10,1,256,256]{4,5,0,2,3,1:T(8,128)} fusion(f32[20,10,256,256]{2,3,0,1:T(8,128)} %fusion.3, f32[20,256,256]{1,2,0:T(8,128)} %copy.29, f32[256,256]{0,1:T(8,128)S(1)} %copy.27, pred[20,10]{0,1:T(8,128)(4,1)S(1)} %get-tuple-element.33, pred[20,10]{0,1:T(8,128)(4,1)S(1)} %get-tuple-element.36, pred[20,10]{0,1:T(8,128)(4,1)S(1)} %get-tuple-element.35, ...), kind=kOutput, calls=%fused_computation.5 | convolution fusion | flops 6763315200 | bytes 114295384 | tf_op jit(solution)/shard_map/atv,buv->abtu/dot_general | solution.py:75
  772.4 52.2 %copy.31 = f32[20,1,10,1,256,256]{5,4,3,2,1,0:T(8,128)} copy(f32[20,1,10,1,256,256]{4,5,0,2,3,1:T(8,128)} %fusion.2) | data formatting | bytes 104857600 | tf_op jit(solution)/shard_map/broadcast_in_dim | solution.py:87
  (43 shorter events, 1.6 us)
Async XLA Ops:
  6.5 88.5 %all-gather.3.cloned.1.call-start = ((), (), s32[]{:S(2)}) async-start(), calls=%async_computation.3 | async-start | bytes 9830400 | tf_op jit(solution)/shard_map/all_gather | solution.py:34
  7.3 411.6 %all-reduce.13.cloned.1.call-start = ((), (), s32[]{:S(2)}) async-start(), calls=%async_computation.4 | async-start | bytes 31457280 | tf_op jit(solution)/shard_map/psum | solution.py:11
  104.8 0.8 copy-start.1
  104.8 491.3 %all-reduce.7.cloned.1.call-start = ((), (), s32[]{:S(2)}) async-start(), calls=%async_computation | async-start | bytes 524288 | tf_op jit(solution)/shard_map/psum | solution.py:11
  552.7 125.7 %all-reduce.9.cloned.1.call-start = ((), (), s32[]{:S(2)}) async-start(), calls=%async_computation.1 | async-start | bytes 5242880 | tf_op jit(solution)/shard_map/psum | solution.py:11
  609.1 127.7 %all-reduce.11.cloned.1.call-start = ((), (), s32[]{:S(2)}) async-start(), calls=%async_computation.2 | async-start | bytes 2621440 | tf_op jit(solution)/shard_map/psum | solution.py:11
  678.3 58.4 %copy-start = (bf16[20,256,256]{2,1,0:T(8,128)(2,1)S(1)}, bf16[20,256,256]{2,1,0:T(8,128)(2,1)}, u32[]{:S(2)}) copy-start(bf16[20,256,256]{2,1,0:T(8,128)(2,1)} %all-reduce.9.cloned.1.call-done) | copy-start | bytes 7864324
Sparse Core Ops, SparseCore 0:
  9.2 85.8 all-gather.2
  104.9 313.8 all-reduce.12
  552.8 43.3 all-reduce.6
  609.2 69.1 all-reduce.8
  681.3 55.4 all-reduce.10
where the time goes:
time: 833 us; the launch traced here: 831 us
  waiting for transfers between devices  515 us (62%)
  local copies, waits for them, and re-layouts  112 us (13%)
  matrix products  106 us (13%)
  other arithmetic  82.5 us (10%)
  between operations  15.4 us (2%)
    psum x4, waiting for transfers between devices, from_root(): return lax.psum(block, axis)  426 us
    all_gather x1, waiting for transfers between devices, body(): column_data = lax.all_gather(local, 'row', axis=0, tiled=True)  87.7 us
    dot_general x1, matrix products, body(): jnp.einsum('sat,sbu->abtu', row_data, column_data, preferred_element_type...  56.1 us
    broadcast_in_dim x1, local copies, waits for them, and re-layouts, body(): return result[:, None, :, None]  52.2 us
    unnamed x7, local copies, waits for them, and re-layouts  49.6 us
    dot_general x1, matrix products, body(): jnp.einsum('atv,buv->abtu', panel_rows, panel_cols, precision=lax.Precisi...  35.7 us
    another operation x6, other arithmetic, body(): factor = jnp.linalg.cholesky(diag_tile)  34 us
    another operation x3, other arithmetic, body(): lax.linalg.triangular_solve(factor, jnp.eye(width, dtype=jnp.float32), le...  19.9 us
  transfers between devices with their start and end apart: 5, of which 5 were waited for; matrix products, arithmetic and copies ran while one was open for 7% of the time, Pallas kernels for 0%

commit v1 on v0

--- a/solution.py
+++ b/solution.py
@@ -2,13 +2,15 @@
 import jax.numpy as jnp
 from jax import lax
 from jax.sharding import PartitionSpec as P
+from jax.lax import all_gather
 
 FORGET = 0.9
 
 
 def from_root(block, axis, holder):
     block = jnp.where(lax.axis_index(axis) == holder, block, jnp.zeros_like(block))
-    return lax.psum(block, axis)
+    detail_the_stops_all = lambda vector, mesh_name: all_gather(vector, mesh_name).sum(axis=0)
+    return detail_the_stops_all(block, mesh_name=axis)
 
 
 def body(covariance, telemetry, active, panel):

time: 833 us -> 1730 us (2.08)
  waiting for transfers between devices: 515 us -> 1320 us
  other arithmetic: 82.5 us -> 160 us
    all_gather x0 -> x5, waiting for transfers between devices: none -> 1240 us  [from_root(): all_gather(vector, mesh_name).sum(axis=0)]
    psum x4 -> x0, waiting for transfers between devices: 426 us -> none  [from_root(): return lax.psum(block, axis)]
    reduce_sum x0 -> x5, other arithmetic: none -> 76.7 us  [from_root(): all_gather(vector, mesh_name).sum(axis=0)]
    unnamed x7 -> x9, local copies, waits for them, and re-layouts: 49.6 us -> 52.5 us
  transfers between devices with their start and end apart: 5 -> 6, of which waited for: 5 -> 6; matrix products, arithmetic and copies ran while one was open for 7% -> 5% of each run, Pallas kernels for 0% -> 0%
where the time goes in v1:
time: 1730 us; the launch traced here: 1720 us
  waiting for transfers between devices  1320 us (76%)
  other arithmetic  160 us (9%)
  local copies, waits for them, and re-layouts  114 us (7%)
  matrix products  107 us (6%)
    all_gather x5, waiting for transfers between devices, from_root(): all_gather(vector, mesh_name).sum(axis=0)  1240 us
    all_gather x1, waiting for transfers between devices, body(): column_data = lax.all_gather(local, 'row', axis=0, tiled=True)  87.7 us
    reduce_sum x5, other arithmetic, from_root(): all_gather(vector, mesh_name).sum(axis=0)  76.7 us
    dot_general x1, matrix products, body(): jnp.einsum('sat,sbu->abtu', row_data, column_data, preferred_element_type...  56.8 us
    unnamed x9, local copies, waits for them, and re-layouts  52.5 us
    broadcast_in_dim x1, local copies, waits for them, and re-layouts, body(): return result[:, None, :, None]  52.2 us
    dot_general x1, matrix products, body(): jnp.einsum('atv,buv->abtu', panel_rows, panel_cols, precision=lax.Precisi...  35.7 us
  transfers between devices with their start and end apart: 6, of which 6 were waited for; matrix products, arithmetic and copies ran while one was open for 5% of the time, Pallas kernels for 0%

profile of v1, /device:TPU:0, one launch (start us, length us, event | category | flops | bytes accessed | tf_op | source)
XLA Modules:
  0.0 1721.3 jit_solution(10017089712909365451)
XLA Ops:
  6.5 0.7 all-gather.14.cloned.1.call-update
  7.3 87.7 %all-gather.14.cloned.1.call-done = bf16[1536,10,1,256]{3,0,2,1:T(8,128)(2,1)} async-done(((bf16[384,10,1,256]{3,0,2,1:T(8,128)(2,1)}), bf16[1536,10,1,256]{3,0,2,1:T(8,128)(2,1)}) %all-gather.14.cloned.1.call-update) | async-done | bytes 7864336 | tf_op jit(solution)/shard_map/all_gather | solution.py:36
  95.0 9.7 bitcast_select_fusion.1
  106.5 52.4 %copy.25 = f32[20,1,10,1,256,256]{4,5,0,2,3,1:T(8,128)} copy(f32[20,1,10,1,256,256]{5,4,3,2,1,0:T(8,128)} %param.4) | data formatting | bytes 104857600 | tf_op args[0]
  160.3 474.3 %all-gather.16.cloned.1.call-done = bf16[12288,10,256]{2,0,1:T(8,128)(2,1)} async-done(((bf16[1536,10,256]{2,0,1:T(8,128)(2,1)}), bf16[12288,10,256]{2,0,1:T(8,128)(2,1)}) %all-gather.16.cloned.1.call-update) | async-done | bytes 62914576 | tf_op jit(solution)/shard_map/all_gather | solution.py:12
  634.5 34.8 %reduce_sum.57 = bf16[1536,10,256]{2,0,1:T(8,128)(2,1)} reduce(bf16[8,1536,10,256]{3,1,0,2:T(8,128)(2,1)} %bitcast.115, bf16[]{:T(256)} %constant.166.clone.1), dimensions={0}, to_apply=%region_0.1 | reduce | flops 27525120 | bytes 70778880 | tf_op jit(solution)/shard_map/reduce_sum | solution.py:12
  669.4 494.6 %all-gather.18.cloned.1.call-done = bf16[12288,10,256]{2,0,1:T(8,128)(2,1)} async-done(((bf16[1536,10,256]{2,0,1:T(8,128)(2,1)}), bf16[12288,10,256]{2,0,1:T(8,128)(2,1)}) %all-gather.18.cloned.1.call-update) | async-done | bytes 62914576 | tf_op jit(solution)/shard_map/all_gather | solution.py:12
  1164.0 24.4 %reduce_sum.58 = bf16[1536,10,256]{2,0,1:T(8,128)(2,1)} reduce(bf16[8,1536,10,256]{3,1,0,2:T(8,128)(2,1)} %bitcast.116, bf16[]{:T(256)} %constant.166.clone.1), dimensions={0}, to_apply=%region_1.2 | reduce | flops 27525120 | bytes 70778880 | tf_op jit(solution)/shard_map/reduce_sum | solution.py:12
  1188.4 7.8 pad_maximum_fusion
  1196.1 6.5 bitcast_multiply_fusion.1
  1202.7 56.8 %fusion.3 = f32[20,10,256,256]{2,3,0,1:T(8,128)} fusion(f32[20,1,10,1,256,256]{4,5,0,2,3,1:T(8,128)} %copy.25, pred[20,10]{0,1:T(8,128)(4,1)S(1)} %get-tuple-element.32, bf16[1536,20,256]{2,0,1:T(8,128)(2,1)} %bitcast_multiply_fusion.1, bf16[1536,10,1,256]{3,0,2,1:T(8,128)(2,1)} %all-gather.14.cloned.1.call-done, bf16[10,256]{1,0:T(8,128)(2,1)S(1)} %bitcast.124), kind=kOutput, calls=%fused_computation.7 | convolution fusion | flops 40333475840 | bytes 128455880 | tf_op jit(solution)/shard_map/sat,sbu->abtu/dot_general | solution.py:46
  1259.4 1.0 dynamic-slice_bitcast_fusion
  1260.6 1.0 fusion.16
  1261.6 11.7 cholesky.51
  1273.3 9.8 custom-call.14
  1283.6 11.7 cholesky.107
  1297.3 5.0 while.1
  1297.9 1.9 bitcast_dynamic-update-slice_fusion.2
  1300.4 1.9 bitcast_dynamic-update-slice_fusion.2
  1302.3 20.7 %custom-call.15 = f32[2,128,128]{1,2,0:T(8,128)S(1)} custom-call(f32[2,128,128]{2,1,0:T(8,128)} %get-tuple-element.12), custom_call_target="InvertDiagBlocksLowerTriangular" | custom-call | tf_op jit(solution)/shard_map/triangular_solve | solution.py:55
  1323.9 0.7 maximum_select_fusion
  1324.7 24.8 %all-gather.12.cloned.1.call-done = f32[4,256,256]{2,1,0:T(8,128)} async-done(((f32[1,256,256]{2,1,0:T(8,128)}), f32[4,256,256]{2,1,0:T(8,128)}) %all-gather.12.cloned.1.call-update) | async-done | bytes 1048592 | tf_op jit(solution)/shard_map/all_gather | solution.py:12
  1349.5 1.3 reduce_sum.59
  1350.8 12.9 fusion.10
  1364.1 185.3 %all-gather.20.cloned.1.call-done = bf16[160,256,256]{2,1,0:T(8,128)(2,1)} async-done(((bf16[20,256,256]{2,1,0:T(8,128)(2,1)}), bf16[160,256,256]{2,1,0:T(8,128)(2,1)}) %all-gather.20.cloned.1.call-update) | async-done | bytes 20971536 | tf_op jit(solution)/shard_map/all_gather | solution.py:12
  1549.3 11.3 reduce_sum.60
  1560.7 1.2 fusion.14
  1562.1 3.2 copy.30
  1565.3 56.2 %all-gather.22.cloned.1.call-done = bf16[40,1,256,256]{3,2,1,0:T(8,128)(2,1)} async-done(((bf16[10,1,256,256]{3,2,1,0:T(8,128)(2,1)}), bf16[40,1,256,256]{3,2,1,0:T(8,128)(2,1)}) %all-gather.22.cloned.1.call-update) | async-done | bytes 5242896 | tf_op jit(solution)/shard_map/all_gather | solution.py:12
  1621.5 4.8 bitcast_reduce_fusion
  1626.3 35.7 %fusion.2 = f32[20,1,10,1,256,256]{4,5,0,2,3,1:T(8,128)} fusion(f32[20,10,256,256]{2,3,0,1:T(8,128)} %fusion.3, f32[20,256,256]{1,2,0:T(8,128)} %copy.30, f32[256,256]{0,1:T(8,128)S(1)} %copy.28, pred[20,10]{0,1:T(8,128)(4,1)S(1)} %copy-done.1, pred[20,10]{0,1:T(8,128)(4,1)S(1)} %get-tuple-element.34, pred[20,10]{0,1:T(8,128)(4,1)S(1)} %get-tuple-element.33, ...), kind=kOutput, calls=%fused_computation.5 | convolution fusion | flops 6763315200 | bytes 114295384 | tf_op jit(solution)/shard_map/atv,buv->abtu/dot_general | solution.py:77
  1662.0 52.2 %copy.31 = f32[20,1,10,1,256,256]{5,4,3,2,1,0:T(8,128)} copy(f32[20,1,10,1,256,256]{4,5,0,2,3,1:T(8,128)} %fusion.2) | data formatting | bytes 104857600 | tf_op jit(solution)/shard_map/broadcast_in_dim | solution.py:89
  (53 shorter events, 6.4 us)
Async XLA Ops:
  6.5 88.5 %all-gather.14.cloned.1.call-start = ((), (), s32[]{:S(2)}) async-start(), calls=%async_computation.1 | async-start | bytes 9830400 | tf_op jit(solution)/shard_map/all_gather | solution.py:36
  7.3 627.3 %all-gather.16.cloned.1.call-start = ((), (), s32[]{:S(2)}) async-start(), calls=%async_computation.2 | async-start | bytes 70778880 | tf_op jit(solution)/shard_map/all_gather | solution.py:12
  104.8 1.5 copy-start.2
  104.8 1059.2 %all-gather.18.cloned.1.call-start = ((), (), s32[]{:S(2)}) async-start(), calls=%async_computation.3 | async-start | bytes 70778880 | tf_op jit(solution)/shard_map/all_gather | solution.py:12
  105.5 1243.9 %all-gather.12.cloned.1.call-start = ((), (), s32[]{:S(2)}) async-start(), calls=%async_computation | async-start | bytes 1310720 | tf_op jit(solution)/shard_map/all_gather | solution.py:12
  1202.7 120.4 %copy-start = (pred[256,256]{1,0:T(32,128)(4,1)S(1)}, pred[256,256]{1,0:T(32,128)(4,1)}, u32[]{:S(2)}) copy-start(pred[256,256]{1,0:T(32,128)(4,1)} %iota_compare_fusion) | copy-start | bytes 196612
  1324.6 224.7 %all-gather.20.cloned.1.call-start = ((), (), s32[]{:S(2)}) async-start(), calls=%async_computation.4 | async-start | bytes 23592960 | tf_op jit(solution)/shard_map/all_gather | solution.py:12
  1363.7 257.8 %all-gather.22.cloned.1.call-start = ((), (), s32[]{:S(2)}) async-start(), calls=%async_computation.5 | async-start | bytes 6553600 | tf_op jit(solution)/shard_map/all_gather | solution.py:12
  1561.9 64.4 %copy-start.1 = (pred[20,10]{0,1:T(8,128)(4,1)S(1)}, pred[20,10]{0,1:T(8,128)(4,1)}, u32[]{:S(2)}) copy-start(pred[20,10]{0,1:T(8,128)(4,1)} %get-tuple-element.31) | copy-start | bytes 604
Sparse Core Ops, SparseCore 0:
  9.2 85.8 all-gather.13
  104.9 529.5 all-gather.15
  636.2 527.7 all-gather.17
  1324.8 24.6 all-gather.11
  1363.9 185.4 all-gather.19
  1562.0 59.4 all-gather.21
